TPU v7x, 32 devices: a whole 2x2x4 slice. The times are simulated.
32 devices in a mesh: dom: 8 (over z, core), loop: 4 (over y, x).
Axes of the slice: x: 2, y: 2, z: 4, core: 2. Of those that a mesh axis runs over, the one named last changes fastest.
Arguments:
- cotangent: bfloat16 [32768, 256], P(('dom', 'loop')), may hold values from -6 to 6
- preact: bfloat16 [32768, 256], P(('dom', 'loop')), may hold values from -6 to 6
- aggregated: bfloat16 [32768, 256], P(('dom', 'loop')), may hold values from -6 to 6
- weight: bfloat16 [256, 256], replicated, may hold values from -0.375 to 0.375
- tile_values: bfloat16 [20480, 128, 128], P(('dom', 'loop')), as said below
- tile_rows: int32 [32, 640], P(('dom', 'loop')), may hold values from 0 to 31
- tile_cols: int32 [32, 640], P(('dom', 'loop')), may hold values from 0 to 63, as said below
- tile_counts: int32 [32], P(('dom', 'loop')), may hold values from 32 to 640
Outputs:
- node_grad: float32 [32768, 256], P(('dom', 'loop'))
- weight_grad: float32 [256, 256], replicated
Inputs may be any that keep to these rules, and one draw needn't show every extreme that they name: `tile_cols`: the live tiles of one device touch, for every dom index, exactly 4 distinct column blocks, and every tile's column lies among them. `tile_values`: entries are nonnegative.
All inputs are finite; a program needn't handle non-finite values.
Results may differ from a plain program's by a relative error of at most 0.0029.
Values may be sent and summed in bfloat16 or wider, within the bound.
No kernel may reach another device: no remote copies, remote signals or barrier semaphores. Data moves between devices by JAX's collectives and lax.ppermute only.
A program may use at most 192 MiB of HBM per device.

v0:
```python
import math

import jax
import jax.numpy as jnp
from jax import lax
from jax.sharding import PartitionSpec as P


def shards(cotangent, preact, aggregated, weight, tile_values, tile_rows, tile_cols, tile_counts):
    node_rows, width = cotangent.shape
    tile_size = tile_values.shape[1]
    dom_count = lax.axis_size("dom")
    total_nodes = node_rows * dom_count * lax.axis_size("loop")
    local_blocks = node_rows // tile_size
    all_blocks = dom_count * local_blocks
    masked = jnp.where(preact > 0, cotangent, jnp.zeros_like(cotangent))
    weight_term = jnp.dot(aggregated.T, masked, preferred_element_type=jnp.float32) * (
        1.0 / math.sqrt(total_nodes)
    )
    weight_grad = lax.psum(weight_term, ("dom", "loop"))
    projected = jnp.dot(masked, weight.T, preferred_element_type=jnp.float32).astype(jnp.bfloat16)
    partition = lax.all_gather(projected, "loop", axis=0, tiled=True)
    part_blocks = partition.shape[0] // tile_size
    flat_rows = partition.reshape(part_blocks, tile_size * width)
    tile_total = tile_rows.shape[1]
    live = (jnp.arange(tile_total, dtype=jnp.int32) < tile_counts[0]).astype(jnp.float32)
    group_size = math.gcd(tile_total, 64)
    groups = tile_total // group_size
    row_ids = jnp.arange(part_blocks, dtype=jnp.int32)
    col_ids = jnp.arange(all_blocks, dtype=jnp.int32)

    def accumulate(totals, item):
        tile_vals, rows_here, cols_here, alive = item
        row_select = (rows_here[:, None] == row_ids[None, :]).astype(jnp.bfloat16)
        picked = jnp.dot(row_select, flat_rows, preferred_element_type=jnp.float32).astype(
            jnp.bfloat16
        )
        picked = picked.reshape(group_size, tile_size, width)
        terms = jnp.einsum("tij,tif->tjf", tile_vals, picked, preferred_element_type=jnp.float32)
        col_select = (col_ids[:, None] == cols_here[None, :]).astype(jnp.float32) * alive[None, :]
        added = jnp.dot(
            col_select,
            terms.reshape(group_size, tile_size * width),
            precision=lax.Precision.HIGHEST,
        )
        return (totals + added, None)

    start = jnp.zeros((all_blocks, tile_size * width), jnp.float32)
    inputs = (
        tile_values.reshape(groups, group_size, tile_size, tile_size),
        tile_rows[0].reshape(groups, group_size),
        tile_cols[0].reshape(groups, group_size),
        live.reshape(groups, group_size),
    )
    adjoint = lax.scan(accumulate, start, inputs)[0]
    node_grad = lax.psum_scatter(
        adjoint.reshape(all_blocks * tile_size, width), "dom", scatter_dimension=0, tiled=True
    )
    return (node_grad, weight_grad)


def solution(mesh):
    return jax.shard_map(
        shards,
        mesh=mesh,
        in_specs=(
            P(("dom", "loop"), None),
            P(("dom", "loop"), None),
            P(("dom", "loop"), None),
            P(),
            P(("dom", "loop"), None, None),
            P(("dom", "loop"), None),
            P(("dom", "loop"), None),
            P(("dom", "loop")),
        ),
        out_specs=(P(("dom", "loop"), None), P()),
        check_vma=False,
    )
```

profile of v0, /device:TPU:0, one launch (start us, length us, event | category | flops | bytes accessed | tf_op | source)
XLA Modules:
  0.0 424.3 jit_solution(11366280374850735796)
XLA Ops:
  12.9 27.7 %copy.10 = bf16[640,128,128]{1,2,0:T(8,128)(2,1)} copy(bf16[640,128,128]{2,1,0:T(8,128)(2,1)} %param.14) | data formatting | bytes 41943040 | tf_op args[4]
  52.4 265.3 %while.11 = (s32[]{:T(128)}, f32[64,32768]{1,0:T(8,128)}, s32[10,64]{1,0:T(8,128)S(1)}, f32[10,64]{1,0:T(8,128)S(1)}, bf16[10,64,128,128]{2,3,1,0:T(8,128)(2,1)}...) while((s32[]{:T(128)}, f32[64,32768]{1,0:T(8,128)}, ...), condition=%wide.region_1.2_spmd.clone, body=%wide.region_0.1_spmd.clone.sunk | while | flops 2288003072 | bytes 71306096 | solution.py:55
  57.7 8.1 %copy.17 = f32[8,8,128,256]{3,1,2,0:T(8,128)} copy(f32[8,8,128,256]{3,2,1,0:T(8,128)S(1)} %bitcast.43) | data formatting | bytes 16777216 | tf_op jit(solution)/shard_map/while
  65.7 12.1 %convolution_add_fusion.2 = f32[64,32768]{1,0:T(8,128)} fusion(f32[64,32768]{1,0:T(8,128)} %bitcast.44, f32[64,32768]{1,0:T(8,128)} %get-tuple-element.153, pred[]{:T(512)S(6)} %compare.3, f32[64]{0:T(128)S(1)} %fusion.41, s32[64]{0:T(128)S(1)} %get-tuple-element.142), kind=kOutput, calls=%fused_computation.2.clone.1 | convolution fusion | flops 1614815232 | bytes 25166336 | tf_op jit(solution)/shard_map/while/body/eval_jaxpr/dot_general | solution.py:41
  83.1 8.1 %copy.17 = f32[8,8,128,256]{3,1,2,0:T(8,128)} copy(f32[8,8,128,256]{3,2,1,0:T(8,128)S(1)} %bitcast.43) | data formatting | bytes 16777216 | tf_op jit(solution)/shard_map/while
  91.1 13.3 %convolution_add_fusion.2 = f32[64,32768]{1,0:T(8,128)} fusion(f32[64,32768]{1,0:T(8,128)} %bitcast.44, f32[64,32768]{1,0:T(8,128)} %get-tuple-element.153, pred[]{:T(512)S(6)} %compare.3, f32[64]{0:T(128)S(1)} %fusion.41, s32[64]{0:T(128)S(1)} %get-tuple-element.142), kind=kOutput, calls=%fused_computation.2.clone.1 | convolution fusion | flops 1614815232 | bytes 25166336 | tf_op jit(solution)/shard_map/while/body/eval_jaxpr/dot_general | solution.py:41
  109.7 8.1 %copy.17 = f32[8,8,128,256]{3,1,2,0:T(8,128)} copy(f32[8,8,128,256]{3,2,1,0:T(8,128)S(1)} %bitcast.43) | data formatting | bytes 16777216 | tf_op jit(solution)/shard_map/while
  117.8 13.3 %convolution_add_fusion.2 = f32[64,32768]{1,0:T(8,128)} fusion(f32[64,32768]{1,0:T(8,128)} %bitcast.44, f32[64,32768]{1,0:T(8,128)} %get-tuple-element.153, pred[]{:T(512)S(6)} %compare.3, f32[64]{0:T(128)S(1)} %fusion.41, s32[64]{0:T(128)S(1)} %get-tuple-element.142), kind=kOutput, calls=%fused_computation.2.clone.1 | convolution fusion | flops 1614815232 | bytes 25166336 | tf_op jit(solution)/shard_map/while/body/eval_jaxpr/dot_general | solution.py:41
  136.4 8.1 %copy.17 = f32[8,8,128,256]{3,1,2,0:T(8,128)} copy(f32[8,8,128,256]{3,2,1,0:T(8,128)S(1)} %bitcast.43) | data formatting | bytes 16777216 | tf_op jit(solution)/shard_map/while
  144.4 13.3 %convolution_add_fusion.2 = f32[64,32768]{1,0:T(8,128)} fusion(f32[64,32768]{1,0:T(8,128)} %bitcast.44, f32[64,32768]{1,0:T(8,128)} %get-tuple-element.153, pred[]{:T(512)S(6)} %compare.3, f32[64]{0:T(128)S(1)} %fusion.41, s32[64]{0:T(128)S(1)} %get-tuple-element.142), kind=kOutput, calls=%fused_computation.2.clone.1 | convolution fusion | flops 1614815232 | bytes 25166336 | tf_op jit(solution)/shard_map/while/body/eval_jaxpr/dot_general | solution.py:41
  163.0 8.1 %copy.17 = f32[8,8,128,256]{3,1,2,0:T(8,128)} copy(f32[8,8,128,256]{3,2,1,0:T(8,128)S(1)} %bitcast.43) | data formatting | bytes 16777216 | tf_op jit(solution)/shard_map/while
  171.1 13.3 %convolution_add_fusion.2 = f32[64,32768]{1,0:T(8,128)} fusion(f32[64,32768]{1,0:T(8,128)} %bitcast.44, f32[64,32768]{1,0:T(8,128)} %get-tuple-element.153, pred[]{:T(512)S(6)} %compare.3, f32[64]{0:T(128)S(1)} %fusion.41, s32[64]{0:T(128)S(1)} %get-tuple-element.142), kind=kOutput, calls=%fused_computation.2.clone.1 | convolution fusion | flops 1614815232 | bytes 25166336 | tf_op jit(solution)/shard_map/while/body/eval_jaxpr/dot_general | solution.py:41
  189.7 8.1 %copy.17 = f32[8,8,128,256]{3,1,2,0:T(8,128)} copy(f32[8,8,128,256]{3,2,1,0:T(8,128)S(1)} %bitcast.43) | data formatting | bytes 16777216 | tf_op jit(solution)/shard_map/while
  197.8 13.3 %convolution_add_fusion.2 = f32[64,32768]{1,0:T(8,128)} fusion(f32[64,32768]{1,0:T(8,128)} %bitcast.44, f32[64,32768]{1,0:T(8,128)} %get-tuple-element.153, pred[]{:T(512)S(6)} %compare.3, f32[64]{0:T(128)S(1)} %fusion.41, s32[64]{0:T(128)S(1)} %get-tuple-element.142), kind=kOutput, calls=%fused_computation.2.clone.1 | convolution fusion | flops 1614815232 | bytes 25166336 | tf_op jit(solution)/shard_map/while/body/eval_jaxpr/dot_general | solution.py:41
  216.3 8.1 %copy.17 = f32[8,8,128,256]{3,1,2,0:T(8,128)} copy(f32[8,8,128,256]{3,2,1,0:T(8,128)S(1)} %bitcast.43) | data formatting | bytes 16777216 | tf_op jit(solution)/shard_map/while
  224.4 13.3 %convolution_add_fusion.2 = f32[64,32768]{1,0:T(8,128)} fusion(f32[64,32768]{1,0:T(8,128)} %bitcast.44, f32[64,32768]{1,0:T(8,128)} %get-tuple-element.153, pred[]{:T(512)S(6)} %compare.3, f32[64]{0:T(128)S(1)} %fusion.41, s32[64]{0:T(128)S(1)} %get-tuple-element.142), kind=kOutput, calls=%fused_computation.2.clone.1 | convolution fusion | flops 1614815232 | bytes 25166336 | tf_op jit(solution)/shard_map/while/body/eval_jaxpr/dot_general | solution.py:41
  243.0 8.1 %copy.17 = f32[8,8,128,256]{3,1,2,0:T(8,128)} copy(f32[8,8,128,256]{3,2,1,0:T(8,128)S(1)} %bitcast.43) | data formatting | bytes 16777216 | tf_op jit(solution)/shard_map/while
  251.1 13.3 %convolution_add_fusion.2 = f32[64,32768]{1,0:T(8,128)} fusion(f32[64,32768]{1,0:T(8,128)} %bitcast.44, f32[64,32768]{1,0:T(8,128)} %get-tuple-element.153, pred[]{:T(512)S(6)} %compare.3, f32[64]{0:T(128)S(1)} %fusion.41, s32[64]{0:T(128)S(1)} %get-tuple-element.142), kind=kOutput, calls=%fused_computation.2.clone.1 | convolution fusion | flops 1614815232 | bytes 25166336 | tf_op jit(solution)/shard_map/while/body/eval_jaxpr/dot_general | solution.py:41
  269.6 8.1 %copy.17 = f32[8,8,128,256]{3,1,2,0:T(8,128)} copy(f32[8,8,128,256]{3,2,1,0:T(8,128)S(1)} %bitcast.43) | data formatting | bytes 16777216 | tf_op jit(solution)/shard_map/while
  277.7 13.3 %convolution_add_fusion.2 = f32[64,32768]{1,0:T(8,128)} fusion(f32[64,32768]{1,0:T(8,128)} %bitcast.44, f32[64,32768]{1,0:T(8,128)} %get-tuple-element.153, pred[]{:T(512)S(6)} %compare.3, f32[64]{0:T(128)S(1)} %fusion.41, s32[64]{0:T(128)S(1)} %get-tuple-element.142), kind=kOutput, calls=%fused_computation.2.clone.1 | convolution fusion | flops 1614815232 | bytes 25166336 | tf_op jit(solution)/shard_map/while/body/eval_jaxpr/dot_general | solution.py:41
  296.3 8.1 %copy.17 = f32[8,8,128,256]{3,1,2,0:T(8,128)} copy(f32[8,8,128,256]{3,2,1,0:T(8,128)S(1)} %bitcast.43) | data formatting | bytes 16777216 | tf_op jit(solution)/shard_map/while
  304.4 13.3 %convolution_add_fusion.2 = f32[64,32768]{1,0:T(8,128)} fusion(f32[64,32768]{1,0:T(8,128)} %bitcast.44, f32[64,32768]{1,0:T(8,128)} %get-tuple-element.153, pred[]{:T(512)S(6)} %compare.3, f32[64]{0:T(128)S(1)} %fusion.41, s32[64]{0:T(128)S(1)} %get-tuple-element.142), kind=kOutput, calls=%fused_computation.2.clone.1 | convolution fusion | flops 1614815232 | bytes 25166336 | tf_op jit(solution)/shard_map/while/body/eval_jaxpr/dot_general | solution.py:41
  317.7 9.3 %reshape.27 = f32[8192,256]{1,0:T(8,128)} reshape(f32[64,32768]{1,0:T(8,128)} %get-tuple-element.49) | data formatting | bytes 16777216 | tf_op jit(solution)/shard_map/reshape | solution.py:57
  328.9 87.9 %reduce-scatter.2.cloned.1.call-done = f32[1024,256]{1,0:T(8,128)} async-done(((f32[8192,256]{1,0:T(8,128)}), f32[1024,256]{1,0:T(8,128)}) %reduce-scatter.2.cloned.1.call-update) | async-done | bytes 1048592 | tf_op jit(solution)/shard_map/reduce_scatter | solution.py:56
  (76 shorter events, 70.3 us)
Async XLA Ops:
  8.0 2.5 copy-start
  8.0 41.5 %all-gather.2.cloned.1.call-start = ((), (), s32[]{:S(2)}) async-start(), calls=%async_computation.1 | async-start | bytes 2621440 | tf_op jit(solution)/shard_map/all_gather | solution.py:22
  10.5 316.6 %all-reduce.2.cloned.1.call-start = ((), (), s32[]{:S(2)}) async-start(), calls=%async_computation.3 | async-start | bytes 524288 | tf_op jit(solution)/shard_map/psum | solution.py:20
  12.9 403.9 %reduce-scatter.2.cloned.1.call-start = ((), (), s32[]{:S(2)}) async-start(), calls=%async_computation.2 | async-start | bytes 9437184 | tf_op jit(solution)/shard_map/reduce_scatter | solution.py:56
  12.9 27.7 %copy-start.2 = (s32[1,640]{1,0:T(1,128)S(1)}, s32[1,640]{1,0:T(1,128)}, u32[]{:S(2)}) copy-start(s32[1,640]{1,0:T(1,128)} %param.16) | copy-start | bytes 7684
  12.9 27.8 %copy-start.3 = (s32[1,640]{1,0:T(1,128)S(1)}, s32[1,640]{1,0:T(1,128)}, u32[]{:S(2)}) copy-start(s32[1,640]{1,0:T(1,128)} %param.15) | copy-start | bytes 7684
  317.7 99.1 %copy-start.1 = (bf16[1024,256]{1,0:T(8,128)(2,1)S(1)}, bf16[1024,256]{1,0:T(8,128)(2,1)}, u32[]{:S(2)}) copy-start(bf16[1024,256]{1,0:T(8,128)(2,1)} %param.12) | copy-start | bytes 1572868
Sparse Core Ops, SparseCore 0:
  11.3 38.1 all-gather.1
  327.2 89.5 reduce-scatter.1
Sparse Core Ops, SparseCore 1:
  17.0 137.6 all-reduce.1
where the time goes:
time: 426 us; the launch traced here: 424 us
  matrix products  178 us (42%)
  local copies, waits for them, and re-layouts  134 us (31%)
  waiting for transfers between devices  96 us (23%)
  between operations  16.2 us (4%)
    dot_general x10, matrix products, accumulate(): jnp.dot(col_select, terms.reshape(group_size, tile_size * width), precisi...  132 us
    while x20, local copies, waits for them, and re-layouts  91.6 us
    reduce_scatter x1, waiting for transfers between devices, shards(): lax.psum_scatter(adjoint.reshape(all_blocks * tile_size, width), 'dom', s...  87.9 us
    unnamed x10, local copies, waits for them, and re-layouts  29.5 us
    dot_general x10, matrix products, accumulate(): jnp.einsum('tij,tif->tjf', tile_vals, picked, preferred_element_type=jnp....  28.5 us
    dot_general x10, matrix products, accumulate(): jnp.dot(row_select, flat_rows, preferred_element_type=jnp.float32)  12.9 us
    reshape x1, local copies, waits for them, and re-layouts, shards(): adjoint.reshape(all_blocks * tile_size, width)  9.34 us
  transfers between devices with their start and end apart: 3, of which 2 were waited for; matrix products, arithmetic and copies ran while one was open for 73% of the time, Pallas kernels for 0%

commit v1 on v0

v1 whole, which is shorter than its diff:
```python
import math

import jax
import jax.numpy as jnp
from jax import lax
from jax.experimental import pallas as pl
from jax.experimental.pallas import tpu as pltpu
from jax.sharding import PartitionSpec as P

GROUP = 32


def _spmm_kernel(rows_ref, cols_ref, cnt_ref, tv_ref, part_ref, out_ref):
    g = pl.program_id(0)
    count = cnt_ref[0]
    group = tv_ref.shape[0]
    base = g * group

    @pl.when(g == 0)
    def _():
        out_ref[...] = jnp.zeros(out_ref.shape, out_ref.dtype)

    @pl.when(base < count)
    def _():
        def body(t, carry):
            j = base + t

            @pl.when(j < count)
            def _():
                r = rows_ref[j]
                c = cols_ref[j]
                term = lax.dot_general(
                    tv_ref[t],
                    part_ref[r],
                    (((0,), (0,)), ((), ())),
                    preferred_element_type=jnp.float32,
                )
                out_ref[c] += term

            return carry

        lax.fori_loop(0, group, body, 0)


def _spmm(rows, cols, count, tile_values, partition, out_blocks):
    tiles, tile_size, _ = tile_values.shape
    part_blocks, _, width = partition.shape
    group = math.gcd(tiles, GROUP)

    def tv_map(g, rows_ref, cols_ref, cnt_ref):
        last = jnp.maximum((cnt_ref[0] + group - 1) // group - 1, 0)
        return (jnp.minimum(g, last), 0, 0)

    def whole(g, rows_ref, cols_ref, cnt_ref):
        return (0, 0, 0)

    return pl.pallas_call(
        _spmm_kernel,
        out_shape=jax.ShapeDtypeStruct((out_blocks, tile_size, width), jnp.float32),
        grid_spec=pltpu.PrefetchScalarGridSpec(
            num_scalar_prefetch=3,
            grid=(tiles // group,),
            in_specs=[
                pl.BlockSpec((group, tile_size, tile_size), tv_map),
                pl.BlockSpec((part_blocks, tile_size, width), whole),
            ],
            out_specs=pl.BlockSpec((out_blocks, tile_size, width), whole),
        ),
        compiler_params=pltpu.CompilerParams(
            dimension_semantics=("arbitrary",),
            vmem_limit_bytes=100 * 1024 * 1024 // 2,
        ),
    )(rows, cols, count, tile_values, partition)


def shards(cotangent, preact, aggregated, weight, tile_values, tile_rows, tile_cols, tile_counts):
    node_rows, width = cotangent.shape
    tile_size = tile_values.shape[1]
    dom_count = lax.axis_size("dom")
    total_nodes = node_rows * dom_count * lax.axis_size("loop")
    local_blocks = node_rows // tile_size
    all_blocks = dom_count * local_blocks
    masked = jnp.where(preact > 0, cotangent, jnp.zeros_like(cotangent))
    weight_term = jnp.dot(aggregated.T, masked, preferred_element_type=jnp.float32) * (
        1.0 / math.sqrt(total_nodes)
    )
    weight_grad = lax.psum(weight_term, ("dom", "loop"))
    projected = jnp.dot(masked, weight.T, preferred_element_type=jnp.float32).astype(jnp.bfloat16)
    partition = lax.all_gather(projected, "loop", axis=0, tiled=True)
    part_blocks = partition.shape[0] // tile_size
    partition = partition.reshape(part_blocks, tile_size, width)
    adjoint = _spmm(tile_rows[0], tile_cols[0], tile_counts, tile_values, partition, all_blocks)
    node_grad = lax.psum_scatter(
        adjoint.reshape(all_blocks * tile_size, width), "dom", scatter_dimension=0, tiled=True
    )
    return (node_grad, weight_grad)


def solution(mesh):
    return jax.shard_map(
        shards,
        mesh=mesh,
        in_specs=(
            P(("dom", "loop"), None),
            P(("dom", "loop"), None),
            P(("dom", "loop"), None),
            P(),
            P(("dom", "loop"), None, None),
            P(("dom", "loop"), None),
            P(("dom", "loop"), None),
            P(("dom", "loop")),
        ),
        out_specs=(P(("dom", "loop"), None), P()),
        check_vma=False,
    )
```

time: 426 us -> 279 us (0.65)
  matrix products: 178 us -> 4.7 us
  local copies, waits for them, and re-layouts: 134 us -> 3.39 us
  Pallas kernels: 0 us -> 98.3 us
  waiting for transfers between devices: 96 us -> 155 us
    dot_general x30 -> x0, matrix products: 173 us -> none  [the longest x10 132 us: accumulate(): jnp.dot(col_select, terms.reshape(group_size, tile_size * width), precisi...]
    pallas_call x0 -> x1, Pallas kernels: none -> 98.3 us  [_spmm(): pl.pallas_call(_spmm_kernel, out_shape=jax.ShapeDtypeStruct((out_blocks,...]
    while x20 -> x0, local copies, waits for them, and re-layouts: 91.6 us -> none
    all_gather x1, waiting for transfers between devices: 8.02 us -> 34.5 us  [shards(): partition = lax.all_gather(projected, 'loop', axis=0, tiled=True)]
    reduce_scatter x1, waiting for transfers between devices: 87.9 us -> 114 us  [shards(): lax.psum_scatter(adjoint.reshape(all_blocks * tile_size, width), 'dom', s...]
    unnamed x10 -> x5, local copies, waits for them, and re-layouts: 29.5 us -> 3.39 us
    reshape x2 -> x0, local copies, waits for them, and re-layouts: 12.2 us -> none  [the longest x1 9.34 us: shards(): adjoint.reshape(all_blocks * tile_size, width)]
    psum x1, waiting for transfers between devices: 0.03 us -> 6.21 us  [shards(): weight_grad = lax.psum(weight_term, ('dom', 'loop'))]
  transfers between devices with their start and end apart: 3 -> 3, of which waited for: 2 -> 3; matrix products, arithmetic and copies ran while one was open for 73% -> 2% of each run, Pallas kernels for 0% -> 35%
where the time goes in v1:
time: 279 us
  waiting for transfers between devices  155 us (56%)
  Pallas kernels  98.3 us (35%)
  between operations  16.2 us (6%)
  matrix products  4.7 us (2%)
  local copies, waits for them, and re-layouts  3.39 us (1%)
    reduce_scatter x1, waiting for transfers between devices, shards(): lax.psum_scatter(adjoint.reshape(all_blocks * tile_size, width), 'dom', s...  114 us
    pallas_call x1, Pallas kernels, _spmm(): pl.pallas_call(_spmm_kernel, out_shape=jax.ShapeDtypeStruct((out_blocks,...  98.3 us
    all_gather x1, waiting for transfers between devices, shards(): partition = lax.all_gather(projected, 'loop', axis=0, tiled=True)  34.5 us
    psum x1, waiting for transfers between devices, shards(): weight_grad = lax.psum(weight_term, ('dom', 'loop'))  6.21 us
  transfers between devices with their start and end apart: 3, of which 3 were waited for; matrix products, arithmetic and copies ran while one was open for 2% of the time, Pallas kernels for 35%

profile of v1, /device:TPU:0, one launch (start us, length us, event | category | flops | bytes accessed | tf_op | source)
XLA Modules:
  0.0 279.0 jit_solution(10040572096102123933)
XLA Ops:
  8.0 0.0 copy-start
  8.0 0.0 all-gather.2.cloned.1.call-start
  8.1 2.4 convolution_convert_fusion
  10.5 0.0 all-gather.2.cloned.1.call-update
  10.5 0.0 all-reduce.2.cloned.1.call-start
  10.5 0.0 copy-done
  10.5 2.3 fusion
  12.8 0.0 all-reduce.2.cloned.1.call-update
  12.9 0.0 reduce-scatter.2.cloned.1.call-start
  12.9 0.7 reduce.rows_ref
  13.6 0.7 reduce.1.cols_ref
  15.0 34.5 %all-gather.2.cloned.1.call-done = bf16[4096,256]{1,0:T(8,128)(2,1)} async-done(((bf16[1024,256]{1,0:T(8,128)(2,1)}), bf16[4096,256]{1,0:T(8,128)(2,1)}) %all-gather.2.cloned.1.call-update) | async-done | bytes 2097168 | tf_op jit(solution)/shard_map/all_gather | solution.py:89
  49.5 0.0 copy-start.1
  49.5 1.6 copy-done.1
  51.1 98.3 %shard_map.95 = f32[64,128,256]{2,1,0:T(8,128)} custom-call(s32[640]{0:T(1024)S(1)} %reduce.rows_ref, s32[640]{0:T(1024)S(1)} %reduce.1.cols_ref, s32[1]{0:T(128)S(6)} %copy.12.cnt_ref, bf16[640,128,128]{2,1,0:T(8,128)(2,1)} %tv_ref.1, bf16[32,128,256]{2,1,0:T(8,128)(2,1)S(1)} %bitcast.6), custom_call_target="tpu_custom_call" | custom-call | tf_op jit(solution)/shard_map/pallas_call | solution.py:57
  149.4 0.0 reduce-scatter.2.cloned.1.call-update
  149.4 6.2 %all-reduce.2.cloned.1.call-done = f32[256,256]{0,1:T(8,128)} async-done(((f32[256,256]{0,1:T(8,128)}), f32[256,256]{0,1:T(8,128)}) %all-reduce.2.cloned.1.call-update) | async-done | bytes 262160 | tf_op jit(solution)/shard_map/psum | solution.py:87
  155.6 1.8 copy.10
  157.4 114.1 %reduce-scatter.2.cloned.1.call-done = f32[1024,256]{1,0:T(8,128)} async-done(((f32[8192,256]{1,0:T(8,128)}), f32[1024,256]{1,0:T(8,128)}) %reduce-scatter.2.cloned.1.call-update) | async-done | bytes 1048592 | tf_op jit(solution)/shard_map/reduce_scatter | solution.py:93
Async XLA Ops:
  8.0 2.5 copy-start
  8.0 41.5 %all-gather.2.cloned.1.call-start = ((), (), s32[]{:S(2)}) async-start(), calls=%async_computation.1 | async-start | bytes 2621440 | tf_op jit(solution)/shard_map/all_gather | solution.py:89
  10.5 145.2 %all-reduce.2.cloned.1.call-start = ((), (), s32[]{:S(2)}) async-start(), calls=%async_computation.3 | async-start | bytes 524288 | tf_op jit(solution)/shard_map/psum | solution.py:87
  12.9 258.7 %reduce-scatter.2.cloned.1.call-start = ((), (), s32[]{:S(2)}) async-start(), calls=%async_computation.2 | async-start | bytes 9437184 | tf_op jit(solution)/shard_map/reduce_scatter | solution.py:93
  49.5 1.6 copy-start.1
Sparse Core Ops, SparseCore 0:
  11.3 38.1 all-gather.1
  149.6 121.9 reduce-scatter.1
Sparse Core Ops, SparseCore 1:
  17.0 138.5 all-reduce.1
